TPU v7x, 128 devices: a whole 4x4x4 slice. The times are simulated.
128 devices in a mesh: sec: 2 (over y_hi), seq: 8 (over x, core), trk: 8 (over y_lo, z).
Axes of the slice: x: 4, y: 4 (y_hi: 2, y_lo: 2; y = y_hi * 2 + y_lo), z: 4, core: 2. Of those that a mesh axis runs over, the one named last changes fastest.
Arguments:
- tokens: bfloat16 [8, 512, 1536], P('sec', 'seq'), may hold values from -6 to 6
- norm_gain: bfloat16 [1536], replicated, may hold values from 0.25 to 1.75
- dilated_conv_weight: bfloat16 [1536, 3, 1536], P(None, None, 'trk'), may hold values from -0.09375 to 0.09375
- head_weight: bfloat16 [1536, 8, 20, 128], P(None, 'trk'), may hold values from -0.15625 to 0.15625
- targets: bfloat16 [8, 512, 8, 20, 128], P('sec', 'seq', 'trk'), may hold values from 0 to 2
- owner_tiles: int32 [8, 20], P('trk'), may hold values from -1 to 80, as said below
- species: int32 [8], P('sec'), may hold values from 0 to 1, as said below
Outputs:
- conv_grad: float32 [1536, 3, 1536], P(('sec', 'seq'), None, 'trk')
- head_grad: float32 [1536, 8, 20, 128], P(('sec', 'seq'), 'trk')
Inputs may be any that keep to these rules, and one draw needn't show every extreme that they name: `owner_tiles`: each of the 81 tiles (human tiles 0 to 59, then the mouse tiles) stands in exactly one slot of one owner; -1 marks an empty slot; in every draw one owner has all 20 slots filled. `species`: 0 is human, 1 is mouse; exactly half of the samples are mouse.
All inputs are finite; a program needn't handle non-finite values.
Results may differ from a plain program's by a relative error of at most 0.0023.
Values may be sent and summed in bfloat16 or wider, within the bound.
No kernel may reach another device: no remote copies, remote signals or barrier semaphores. Data moves between devices by JAX's collectives and lax.ppermute only.
A program may use at most 128 MiB of HBM per device.

v0:
```python
import math
import jax
import jax.numpy as jnp
from jax import lax
from jax.sharding import PartitionSpec as P

HTRACKS = 7611
MTRACKS = 2608
DILATION_BINS = 16
HTILES = 60
grad_clip = 0.1


def padded(cells, sides, width):
    for axis, dim in sides:
        count = lax.axis_size(axis)
        ends = count - 1
        head = lax.slice_in_dim(cells, 0, width, axis=dim)
        tail = lax.slice_in_dim(cells, cells.shape[dim] - width, cells.shape[dim], axis=dim)
        cells = jnp.concatenate(
            [
                lax.ppermute(tail, axis, [(i, (i + 1) % count) for i in range(ends)]),
                cells,
                lax.ppermute(head, axis, [((i + 1) % count, i) for i in range(ends)]),
            ],
            axis=dim,
        )
    return cells


def contracted_rows(left, right):
    return lax.dot_general(
        left, right, (((0,), (0,)), ((), ())), preferred_element_type=jnp.float32
    )


def body(tokens, norm_gain, dilated_conv_weight, head_weight, targets, owner_tiles, species):
    sample_count = tokens.shape[0]
    local_rows = tokens.shape[1]
    width_all = tokens.shape[2]
    tap_count = dilated_conv_weight.shape[1]
    out_share = dilated_conv_weight.shape[2]
    slot_count = head_weight.shape[2]
    lane_count = head_weight.shape[3]
    inputs = tokens.astype(jnp.float32)
    mean_sq = jnp.mean(inputs * inputs, axis=-1, keepdims=True)
    normed = inputs * lax.rsqrt(mean_sq + 1e-06) * norm_gain.astype(jnp.float32)
    hidden_state = jax.nn.gelu(normed).astype(jnp.bfloat16)
    padded_input = padded(hidden_state, (("seq", 1),), DILATION_BINS)
    convolution_output = jnp.zeros((sample_count, local_rows, out_share), jnp.float32)
    for kernel_tap_index in range(tap_count):
        convolution_output = convolution_output + jnp.dot(
            padded_input[
                :, kernel_tap_index * DILATION_BINS : kernel_tap_index * DILATION_BINS + local_rows
            ],
            dilated_conv_weight[:, kernel_tap_index, :],
            preferred_element_type=jnp.float32,
        )
    own_cols = lax.dynamic_slice_in_dim(inputs, lax.axis_index("trk") * out_share, out_share, 2)
    mixed_share = (own_cols + convolution_output).astype(jnp.bfloat16)
    mixed_all = lax.all_gather(mixed_share, "trk", axis=2, tiled=True)
    tiles_here = owner_tiles[0]
    is_mouse = tiles_here >= HTILES
    within = jnp.where(is_mouse, tiles_here - HTILES, tiles_here)
    track_limit = jnp.where(is_mouse, MTRACKS, HTRACKS).astype(jnp.int32)
    lane_ids = jnp.arange(lane_count, dtype=jnp.int32)
    lane_mask = (within[:, None] * lane_count + lane_ids[None, :] < track_limit[:, None]).astype(
        jnp.float32
    )
    grad_scale = 1.0 / math.sqrt(
        lax.axis_size("sec") * sample_count * lax.axis_size("seq") * local_rows
    )
    weights_here = head_weight[:, 0].reshape(width_all, slot_count * lane_count)
    flat_mixed = mixed_all.reshape(sample_count * local_rows, width_all)
    logits = jnp.dot(flat_mixed, weights_here, preferred_element_type=jnp.float32)
    target_cols = targets[:, :, 0].reshape(sample_count * local_rows, slot_count * lane_count)
    active = (tiles_here[None, :] >= 0) & (is_mouse[None, :] == (species[:, None] == 1))
    live_mask = active.astype(jnp.float32)[:, :, None] * lane_mask[None, :, :]
    live_rows = jnp.broadcast_to(
        live_mask.reshape(sample_count, 1, slot_count * lane_count),
        (sample_count, local_rows, slot_count * lane_count),
    ).reshape(sample_count * local_rows, slot_count * lane_count)
    delta_f = (
        grad_scale
        * (jax.nn.softplus(logits) - target_cols.astype(jnp.float32))
        * jax.nn.sigmoid(logits)
        * live_rows
    )
    flat_deltas = delta_f.astype(jnp.bfloat16)
    back_sum = lax.dot_general(
        flat_deltas, weights_here, (((1,), (1,)), ((), ())), preferred_element_type=jnp.float32
    ).reshape(sample_count, local_rows, width_all)
    backward_portion = lax.psum_scatter(back_sum, "trk", scatter_dimension=2, tiled=True).astype(
        jnp.bfloat16
    )
    group_count = lax.axis_size("sec") * lax.axis_size("seq")
    share_rows = width_all // group_count
    per_tap = [
        lax.dot_general(
            padded_input[
                :, kernel_tap_index * DILATION_BINS : kernel_tap_index * DILATION_BINS + local_rows
            ],
            backward_portion,
            (((0, 1), (0, 1)), ((), ())),
            preferred_element_type=jnp.float32,
        )
        for kernel_tap_index in range(tap_count)
    ]
    conv_grad = lax.psum_scatter(
        jnp.stack(per_tap, axis=1), ("sec", "seq"), scatter_dimension=0, tiled=True
    )
    grad_share = lax.psum_scatter(
        contracted_rows(flat_mixed, flat_deltas), ("sec", "seq"), scatter_dimension=0, tiled=True
    )
    total_sq = lax.psum(jnp.sum(grad_share * grad_share), ("sec", "seq", "trk"))
    entries = width_all * lax.axis_size("trk") * slot_count * lane_count
    factor = jnp.minimum(1.0, grad_clip * lax.rsqrt(total_sq / entries + 1e-06))
    head_grad = (grad_share * factor).reshape(share_rows, 1, slot_count, lane_count)
    return (conv_grad, head_grad)


def solution(mesh):
    return jax.shard_map(
        body,
        mesh=mesh,
        in_specs=(
            P("sec", "seq", None),
            P(),
            P(None, None, "trk"),
            P(None, "trk", None, None),
            P("sec", "seq", "trk", None, None),
            P("trk", None),
            P("sec"),
        ),
        out_specs=(P(("sec", "seq"), None, "trk"), P(("sec", "seq"), "trk", None, None)),
        check_vma=False,
    )
```

profile of v0, /device:TPU:1, one launch (start us, length us, event | category | flops | bytes accessed | tf_op | source)
XLA Modules:
  0.0 435.4 jit_solution(13732311764783962784)
XLA Ops:
  7.2 0.0 copy-start.2
  7.2 0.0 copy-start.7
  7.2 0.0 reduce-scatter.10.cloned.1.call-start
  7.2 1.4 multiply_reduce_fusion
  8.7 0.7 convert_element_type.39
  9.4 1.8 fusion.12
  11.2 0.8 fusion.33
  12.0 4.5 %collective-permute-start = (bf16[4,16,1536]{2,1,0:T(8,128)(2,1)}, bf16[4,16,1536]{2,1,0:T(8,128)(2,1)S(1)}, u32[]{:S(2)}, u32[]{:S(2)}) collective-permute-start(bf16[4,16,1536]{2,1,0:T(8,128)(2,1)} %get-tuple-element.10), channel_id=1, source_target_pairs={{0,8},{8,16},{16,24},{24,32},{32,40},{40,48},{48,56},{1,9},{9,17},... | collective-permute-start | bytes 589832 | tf_op jit(solution)/shard_map/ppermute | solution.py:22
  16.5 1.9 collective-permute-start.1
  18.4 0.0 copy-done.7
  18.4 0.0 copy-done.2
  18.4 0.2 convert_element_type.38
  18.6 0.7 broadcast_compare_fusion
  19.3 0.1 and_convert_fusion
  19.4 0.1 broadcast_bitcast_fusion
  19.5 3.8 copy.26
  23.3 10.6 %copy.25 = bf16[1536,1,20,128]{0,3,2,1:T(8,128)(2,1)} copy(bf16[1536,1,20,128]{3,0,2,1:T(8,128)(2,1)} %param.10) | data formatting | bytes 15728640 | tf_op args[3]
  33.9 0.0 copy-start.6
  33.9 0.1 broadcast_reduce_fusion
  34.1 0.6 bitcast_multiply_fusion
  34.7 1.4 fusion.18
  36.1 0.0 collective-permute-done.1
  36.1 0.0 copy-done.6
  36.1 0.4 fusion.16
  36.5 0.0 collective-permute-done
  36.6 0.4 fusion.15
  36.9 0.2 copy.23
  37.1 29.0 %all_gather.3 = bf16[4,64,1536]{1,0,2:T(4,128)(2,1)S(1)} all-gather(bf16[4,64,192]{1,0,2:T(4,128)(2,1)S(1)} %copy.23), channel_id=1, replica_groups=mesh['sec'=2,'seq'=8,'trk'=8] {'trk'}, dimensions={2}, use_global_device_ids=true | all-gather | bytes 884736 | tf_op jit(solution)/shard_map/all_gather | solution.py:61
  66.1 0.9 copy.24
  67.0 0.0 copy-start
  67.0 8.5 %fusion.4 = bf16[256,2560]{1,0:T(8,128)(2,1)S(1)} fusion(f32[32,8,20,128]{3,2,1,0:T(8,128)} %bitcast.78, f32[4,2560]{1,0:T(4,128)} %bitcast_multiply_fusion, bf16[256,1536]{1,0:T(8,128)(2,1)S(1)} %bitcast.79, bf16[1536,2560]{0,1:T(8,128)(2,1)} %bitcast.74), kind=kOutput, calls=%fused_computation.6 | convolution fusion | flops 2022440960 | bytes 12623872 | tf_op jit(solution)/shard_map/dot_general | solution.py:75
  75.5 0.0 copy-done
  75.5 0.0 copy-start.3
  75.5 1.2 copy-done.3
  76.7 5.4 %fusion.34 = f32[4,64,1536]{2,1,0:T(8,128)S(1)} fusion(bf16[4,64,2560]{2,1,0:T(8,128)(2,1)S(1)} %bitcast.81, bf16[1536,2560,1]{0,1,2:T(8,128)(2,1)} %bitcast.75), kind=kOutput, calls=%fused_computation.59 | convolution fusion | flops 2013265920 | bytes 10747904 | tf_op jit(solution)/shard_map/dot_general | solution.py:90
  82.1 2.7 copy.32
  84.9 4.2 reshape.148
  89.0 0.0 reduce-scatter.10.cloned.1.call-update
  89.1 0.0 reduce-scatter.12.cloned.1.call-start
  89.1 41.3 %reduce-scatter.10.cloned.1.call-done = f32[192,256]{1,0:T(8,128)} async-done(((f32[1536,256]{1,0:T(8,128)}), f32[192,256]{1,0:T(8,128)}) %reduce-scatter.10.cloned.1.call-update) | async-done | bytes 196624
  130.4 1.1 reshape.149
  131.5 0.1 copy.33
  131.6 0.4 convolution_bitcast_fusion.1
  132.0 0.4 convolution_bitcast_fusion
  132.3 0.4 convolution_bitcast_fusion.2
  132.7 0.2 pad_maximum_fusion
  132.9 3.1 copy.36
  136.0 0.0 copy-start.1
  136.0 0.0 copy-start.4
  136.0 0.0 reduce-scatter.12.cloned.1.call-update
  136.1 0.2 reduce-scatter.8.cloned.1.call-start
  136.3 0.9 copy-done.1
  137.2 0.4 copy-done.4
  137.6 7.7 %fusion.35 = f32[1536,2560]{1,0:T(8,128)} fusion(bf16[256,1536]{1,0:T(8,128)(2,1)S(1)} %bitcast.80, bf16[256,2560]{1,0:T(8,128)(2,1)S(1)} %copy-done.4), kind=kOutput, calls=%fused_computation.60 | convolution fusion | flops 2013265920 | bytes 17825792 | tf_op jit(solution)/shard_map/dot_general | solution.py:32
  145.4 0.0 reduce-scatter.8.cloned.1.call-update
  145.4 71.8 %reduce-scatter.12.cloned.1.call-done = f32[96,576]{1,0:T(8,128)} async-done(((f32[1536,576]{1,0:T(8,128)}), f32[96,576]{1,0:T(8,128)}) %reduce-scatter.12.cloned.1.call-update) | async-done | bytes 221200
  217.2 1.1 copy.37
  218.3 140.2 %reduce-scatter.8.cloned.1.call-done = f32[96,2560]{1,0:T(8,128)} async-done(((f32[1536,2560]{1,0:T(8,128)}), f32[96,2560]{1,0:T(8,128)}) %reduce-scatter.8.cloned.1.call-update) | async-done | bytes 983056 | tf_op jit(solution)/shard_map/reduce_scatter | solution.py:112
  358.4 2.1 multiply_reduce_fusion.1
  360.6 0.9 copy.28
  361.5 64.5 %psum.7 = f32[]{:T(128)} all-reduce(f32[]{:T(128)} %multiply_reduce_fusion.1), channel_id=1, replica_groups=mesh['sec'=2,'seq'=8,'trk'=8] {'sec','seq','trk'}, use_global_device_ids=true, to_apply=%region_5.6 | all-reduce | flops 1 | bytes 8 | tf_op jit(solution)/shard_map/psum | solution.py:115
  426.7 0.0 copy-done.5
  426.7 0.1 broadcast_multiply_fusion
  426.8 2.1 reshape.147
  (5 shorter events, 0.0 us)
Async XLA Ops:
  7.2 11.3 %copy-start.2 = (bf16[4,64,1536]{2,1,0:T(8,128)(2,1)S(1)}, bf16[4,64,1536]{2,1,0:T(8,128)(2,1)}, u32[]{:S(2)}) copy-start(bf16[4,64,1536]{2,1,0:T(8,128)(2,1)} %param.7) | copy-start | bytes 2359300
  7.2 11.2 %copy-start.7 = (s32[1,20]{1,0:T(1,128)S(1)}, s32[1,20]{1,0:T(1,128)}, u32[]{:S(2)}) copy-start(s32[1,20]{1,0:T(1,128)} %param.12) | copy-start | bytes 244
  7.2 123.2 %reduce-scatter.10.cloned.1.call-start = ((), (), s32[]{:S(2)}) async-start(), calls=%async_computation.4 | async-start | bytes 1769472
  12.0 24.6 %collective-permute-start = (bf16[4,16,1536]{2,1,0:T(8,128)(2,1)}, bf16[4,16,1536]{2,1,0:T(8,128)(2,1)S(1)}, u32[]{:S(2)}, u32[]{:S(2)}) collective-permute-start(bf16[4,16,1536]{2,1,0:T(8,128)(2,1)} %get-tuple-element.10), channel_id=1, source_target_pairs={{0,8},{8,16},{16,24},{24,32},{32,40},{40,48},{48,56},{1,9},{9,17},... | collective-permute-start | bytes 589832 | tf_op jit(solution)/shard_map/ppermute | solution.py:22
  16.5 19.7 %collective-permute-start.1 = (bf16[4,16,1536]{2,1,0:T(8,128)(2,1)}, bf16[4,16,1536]{2,1,0:T(8,128)(2,1)S(1)}, u32[]{:S(2)}, u32[]{:S(2)}) collective-permute-start(bf16[4,16,1536]{2,1,0:T(8,128)(2,1)} %get-tuple-element.11), channel_id=1, source_target_pairs={{8,0},{16,8},{24,16},{32,24},{40,32},{48,40},{56,48},{9,1},{17,9},... | collective-permute-start | bytes 589832 | tf_op jit(solution)/shard_map/ppermute | solution.py:24
  33.9 2.2 copy-start.6
  67.0 8.5 %copy-start = (bf16[4,64,1536]{2,1,0:T(8,128)(2,1)}, bf16[4,64,1536]{2,1,0:T(8,128)(2,1)S(1)}, u32[]{:S(2)}) copy-start(bf16[4,64,1536]{2,1,0:T(8,128)(2,1)S(1)} %copy.24) | copy-start | bytes 2359300
  75.5 1.2 copy-start.3
  89.1 128.1 %reduce-scatter.12.cloned.1.call-start = ((), (), s32[]{:S(2)}) async-start(), calls=%async_computation.5 | async-start | bytes 4177920
  136.0 1.1 copy-start.1
  136.0 1.6 copy-start.4
  136.1 222.4 %reduce-scatter.8.cloned.1.call-start = ((), (), s32[]{:S(2)}) async-start(), calls=%async_computation.3 | async-start | bytes 16711680 | tf_op jit(solution)/shard_map/reduce_scatter | solution.py:112
  358.4 68.2 %copy-start.5 = (f32[96,2560]{1,0:T(8,128)S(1)}, f32[96,2560]{1,0:T(8,128)}, u32[]{:S(2)}) copy-start(f32[96,2560]{1,0:T(8,128)} %reduce-scatter.8.cloned.1.call-done) | copy-start | bytes 2949124
Sparse Core Ops, SparseCore 0:
  89.2 41.1 reduce-scatter.9
  136.2 80.9 reduce-scatter.11
  221.6 136.7 reduce-scatter.7
where the time goes:
time: 436 us; the launch traced here: 435 us
  waiting for transfers between devices  253 us (58%)
  blocking collectives  93.5 us (21%)
  local copies, waits for them, and re-layouts  34.3 us (8%)
  matrix products  24.9 us (6%)
  between operations  14.7 us (3%)
  other arithmetic  7.97 us (2%)
  starting transfers between devices  6.71 us (2%)
    reduce_scatter x1, waiting for transfers between devices, body(): lax.psum_scatter(contracted_rows(flat_mixed, flat_deltas), ('sec', 'seq')...  140 us
    unnamed x5, waiting for transfers between devices  113 us
    psum x1, blocking collectives, body(): total_sq = lax.psum(jnp.sum(grad_share * grad_share), ('sec', 'seq', 'trk'))  64.5 us
    all_gather x1, blocking collectives, body(): mixed_all = lax.all_gather(mixed_share, 'trk', axis=2, tiled=True)  29 us
    unnamed x25, local copies, waits for them, and re-layouts  26.4 us
  transfers between devices with their start and end apart: 5, of which 3 were waited for; matrix products, arithmetic and copies ran while one was open for 6% of the time, Pallas kernels for 0%

commit v1 on v0

--- a/solution.py
+++ b/solution.py
@@ -3,6 +3,7 @@
 import jax.numpy as jnp
 from jax import lax
 from jax.sharding import PartitionSpec as P
+from jax.lax import all_to_all, axis_size
 
 HTRACKS = 7611
 MTRACKS = 2608
@@ -58,7 +59,10 @@
         )
     own_cols = lax.dynamic_slice_in_dim(inputs, lax.axis_index("trk") * out_share, out_share, 2)
     mixed_share = (own_cols + convolution_output).astype(jnp.bfloat16)
-    mixed_all = lax.all_gather(mixed_share, "trk", axis=2, tiled=True)
+    mixed_all = jnp.concatenate(
+        all_to_all(jnp.stack([mixed_share for _ in range(axis_size("trk"))], axis=0), "trk", 0, 0),
+        2,
+    )
     tiles_here = owner_tiles[0]
     is_mouse = tiles_here >= HTILES
     within = jnp.where(is_mouse, tiles_here - HTILES, tiles_here)

time: 436 us -> 415 us (0.952)
  blocking collectives: 93.5 us -> 64.4 us
  starting transfers between devices: 6.71 us -> 12.8 us
    all_gather x1 -> x0, blocking collectives: 29 us -> none  [body(): mixed_all = lax.all_gather(mixed_share, 'trk', axis=2, tiled=True)]
    all_to_all x0 -> x1, starting transfers between devices: none -> 6.05 us  [body(): all_to_all(jnp.stack([mixed_share for _ in range(axis_size('trk'))], axis...]
    unnamed x5, waiting for transfers between devices: 113 us -> 109 us
    unnamed x25 -> x31, local copies, waits for them, and re-layouts: 26.4 us -> 28.2 us
  transfers between devices with their start and end apart: 5 -> 6, of which waited for: 3 -> 4; matrix products, arithmetic and copies ran while one was open for 6% -> 7% of each run, Pallas kernels for 0% -> 0%
where the time goes in v1:
time: 415 us; the launch traced here: 414 us
  waiting for transfers between devices  251 us (60%)
  blocking collectives  64.4 us (16%)
  local copies, waits for them, and re-layouts  37.4 us (9%)
  matrix products  27 us (7%)
  between operations  14.7 us (4%)
  starting transfers between devices  12.8 us (3%)
  other arithmetic  7.45 us (2%)
    reduce_scatter x1, waiting for transfers between devices, body(): lax.psum_scatter(contracted_rows(flat_mixed, flat_deltas), ('sec', 'seq')...  140 us
    unnamed x5, waiting for transfers between devices  109 us
    psum x1, blocking collectives, body(): total_sq = lax.psum(jnp.sum(grad_share * grad_share), ('sec', 'seq', 'trk'))  64.4 us
    unnamed x31, local copies, waits for them, and re-layouts  28.2 us
    dot_general x1, matrix products, body(): jnp.dot(flat_mixed, weights_here, preferred_element_type=jnp.float32)  8.41 us
  transfers between devices with their start and end apart: 6, of which 4 were waited for; matrix products, arithmetic and copies ran while one was open for 7% of the time, Pallas kernels for 0%

profile of v1, /device:TPU:1, one launch (start us, length us, event | category | flops | bytes accessed | tf_op | source)
XLA Modules:
  0.0 414.4 jit_solution(247330332789640449)
XLA Ops:
  7.2 0.0 copy-start.2
  7.2 0.0 copy-start.9
  7.2 1.4 multiply_reduce_fusion
  8.6 0.7 convert_element_type.39
  9.3 1.8 fusion.12
  11.2 0.0 copy-start.10
  11.2 4.5 %collective-permute-start = (bf16[4,16,1536]{2,1,0:T(8,128)(2,1)S(1)}, bf16[4,16,1536]{2,1,0:T(8,128)(2,1)S(1)}, u32[]{:S(2)}, u32[]{:S(2)}) collective-permute-start(bf16[4,16,1536]{2,1,0:T(8,128)(2,1)S(1)} %get-tuple-element.8), channel_id=1, source_target_pairs={{0,8},{8,16},{16,24},{24,32},{32,40},{40,48},{48,56},{1,9},{9,17},... | collective-permute-start | bytes 589832 | tf_op jit(solution)/shard_map/ppermute | solution.py:23
  15.7 1.9 collective-permute-start.1
  17.7 0.0 copy-done.9
  17.7 0.0 copy-done.2
  17.7 0.2 convert_element_type.38
  17.9 0.0 copy-done.10
  17.9 1.4 fusion.18
  19.4 0.7 broadcast_reduce_fusion
  20.1 0.1 and_convert_fusion
  20.2 0.7 broadcast_bitcast_fusion
  20.9 1.8 collective-permute-done.1
  22.7 1.4 fusion.16
  24.2 0.0 collective-permute-done
  24.2 1.5 fusion.15
  25.6 0.0 copy-start.7
  25.7 1.1 stack.10
  26.8 6.0 %all-to-all-start = ((bf16[8,4,64,192]{3,2,1,0:T(8,128)(2,1)}), bf16[8,4,64,192]{3,2,1,0:T(8,128)(2,1)S(1)}, u32[]{:S(2)}, u32[]{:S(2)}) async-start(bf16[8,4,64,192]{3,2,1,0:T(8,128)(2,1)} %stack.10), calls=%async_computation | async-start | bytes 2097152 | tf_op jit(solution)/shard_map/all_to_all | solution.py:63
  32.8 0.0 reduce-scatter.10.cloned.1.call-start
  32.9 0.7 fusion.24
  33.6 0.0 copy-done.7
  33.6 2.5 copy.19
  36.1 10.6 %copy.18 = bf16[1536,1,20,128]{0,3,2,1:T(8,128)(2,1)} copy(bf16[1536,1,20,128]{3,0,2,1:T(8,128)(2,1)} %param.10) | data formatting | bytes 15728640 | tf_op args[3]
  46.8 0.0 copy-done.8
  46.8 0.0 all-to-all-done
  46.8 0.0 copy-start.5
  46.8 1.0 copy-done.5
  47.8 1.8 copy.17
  49.6 0.9 reshape_reshape.3
  50.5 0.0 copy-start
  50.5 8.4 %fusion.4 = bf16[256,2560]{1,0:T(8,128)(2,1)S(1)} fusion(f32[32,8,20,128]{3,2,1,0:T(8,128)} %bitcast.80, f32[4,2560]{1,0:T(4,128)S(1)} %bitcast_multiply_fusion, bf16[256,1536]{1,0:T(8,128)(2,1)S(1)} %reshape_reshape.3, bf16[1536,2560]{0,1:T(8,128)(2,1)} %bitcast.76), kind=kOutput, calls=%fused_computation.6 | convolution fusion | flops 2022440960 | bytes 12623872 | tf_op jit(solution)/shard_map/dot_general | solution.py:79
  59.0 1.2 copy-done.3
  60.1 5.4 %fusion.34 = f32[4,64,1536]{2,1,0:T(8,128)S(1)} fusion(bf16[4,64,2560]{2,1,0:T(8,128)(2,1)S(1)} %bitcast.81, bf16[1536,2560,1]{0,1,2:T(8,128)(2,1)} %bitcast.77), kind=kOutput, calls=%fused_computation.59 | convolution fusion | flops 2013265920 | bytes 10747904 | tf_op jit(solution)/shard_map/dot_general | solution.py:94
  65.6 2.7 copy.25
  68.3 4.2 %reshape.150 = f32[1536,256]{1,0:T(8,128)} reshape(f32[1536,4,64]{2,1,0:T(4,128)} %bitcast.79) | data formatting | bytes 3145728
  72.5 0.0 reduce-scatter.10.cloned.1.call-update
  72.5 0.2 reduce-scatter.12.cloned.1.call-start
  72.7 36.6 %reduce-scatter.10.cloned.1.call-done = f32[192,256]{1,0:T(8,128)} async-done(((f32[1536,256]{1,0:T(8,128)}), f32[192,256]{1,0:T(8,128)}) %reduce-scatter.10.cloned.1.call-update) | async-done | bytes 196624
  109.3 1.1 reshape.151
  110.3 0.1 copy.26
  110.5 0.4 convolution_bitcast_fusion.1
  110.9 0.4 convolution_bitcast_fusion
  111.2 0.4 convolution_bitcast_fusion.2
  111.6 0.2 pad_maximum_fusion
  111.8 3.1 copy.29
  114.9 0.0 reduce-scatter.12.cloned.1.call-update
  115.0 0.0 reduce-scatter.8.cloned.1.call-start
  115.0 1.1 copy-done.1
  116.1 0.4 copy-done.4
  116.5 7.7 %fusion.35 = f32[1536,2560]{1,0:T(8,128)} fusion(bf16[256,1536]{1,0:T(8,128)(2,1)S(1)} %copy-done.1, bf16[256,2560]{1,0:T(8,128)(2,1)S(1)} %copy-done.4), kind=kOutput, calls=%fused_computation.60 | convolution fusion | flops 2013265920 | bytes 17825792 | tf_op jit(solution)/shard_map/dot_general | solution.py:33
  124.2 0.0 reduce-scatter.8.cloned.1.call-update
  124.3 72.0 %reduce-scatter.12.cloned.1.call-done = f32[96,576]{1,0:T(8,128)} async-done(((f32[1536,576]{1,0:T(8,128)}), f32[96,576]{1,0:T(8,128)}) %reduce-scatter.12.cloned.1.call-update) | async-done | bytes 221200
  196.3 1.1 copy.30
  197.4 140.1 %reduce-scatter.8.cloned.1.call-done = f32[96,2560]{1,0:T(8,128)} async-done(((f32[1536,2560]{1,0:T(8,128)}), f32[96,2560]{1,0:T(8,128)}) %reduce-scatter.8.cloned.1.call-update) | async-done | bytes 983056 | tf_op jit(solution)/shard_map/reduce_scatter | solution.py:116
  337.5 2.1 multiply_reduce_fusion.1
  339.6 0.9 copy.21
  340.5 64.4 %psum.7 = f32[]{:T(128)} all-reduce(f32[]{:T(128)} %multiply_reduce_fusion.1), channel_id=1, replica_groups=mesh['sec'=2,'seq'=8,'trk'=8] {'sec','seq','trk'}, use_global_device_ids=true, to_apply=%region_5.6 | all-reduce | flops 1 | bytes 8 | tf_op jit(solution)/shard_map/psum | solution.py:119
  405.7 0.1 broadcast_multiply_fusion
  405.7 2.1 reshape.149
  (13 shorter events, 0.1 us)
Async XLA Ops:
  7.2 10.5 %copy-start.2 = (bf16[4,64,1536]{2,1,0:T(8,128)(2,1)S(1)}, bf16[4,64,1536]{2,1,0:T(8,128)(2,1)}, u32[]{:S(2)}) copy-start(bf16[4,64,1536]{2,1,0:T(8,128)(2,1)} %param.7) | copy-start | bytes 2359300
  7.2 10.5 %copy-start.9 = (s32[1,20]{1,0:T(1,128)S(1)}, s32[1,20]{1,0:T(1,128)}, u32[]{:S(2)}) copy-start(s32[1,20]{1,0:T(1,128)} %param.12) | copy-start | bytes 244
  11.2 6.7 %copy-start.10 = (s32[4]{0:T(128)S(1)}, s32[4]{0:T(128)}, u32[]{:S(2)}) copy-start(s32[4]{0:T(128)} %param.13) | copy-start | bytes 52
  11.2 12.9 %collective-permute-start = (bf16[4,16,1536]{2,1,0:T(8,128)(2,1)S(1)}, bf16[4,16,1536]{2,1,0:T(8,128)(2,1)S(1)}, u32[]{:S(2)}, u32[]{:S(2)}) collective-permute-start(bf16[4,16,1536]{2,1,0:T(8,128)(2,1)S(1)} %get-tuple-element.8), channel_id=1, source_target_pairs={{0,8},{8,16},{16,24},{24,32},{32,40},{40,48},{48,56},{1,9},{9,17},... | collective-permute-start | bytes 589832 | tf_op jit(solution)/shard_map/ppermute | solution.py:23
  15.7 7.0 %collective-permute-start.1 = (bf16[4,16,1536]{2,1,0:T(8,128)(2,1)S(1)}, bf16[4,16,1536]{2,1,0:T(8,128)(2,1)S(1)}, u32[]{:S(2)}, u32[]{:S(2)}) collective-permute-start(bf16[4,16,1536]{2,1,0:T(8,128)(2,1)S(1)} %get-tuple-element.9), channel_id=1, source_target_pairs={{8,0},{16,8},{24,16},{32,24},{40,32},{48,40},{56,48},{9,1},{17,9},... | collective-permute-start | bytes 589832 | tf_op jit(solution)/shard_map/ppermute | solution.py:25
  25.6 7.9 %copy-start.7 = (bf16[4,64,1,20,128]{4,1,3,2,0:T(8,128)(2,1)S(1)}, bf16[4,64,1,20,128]{4,1,3,2,0:T(8,128)(2,1)}, u32[]{:S(2)}) copy-start(bf16[4,64,1,20,128]{4,1,3,2,0:T(8,128)(2,1)} %param.11) | copy-start | bytes 3932164
  26.8 20.0 %all-to-all-start = ((bf16[8,4,64,192]{3,2,1,0:T(8,128)(2,1)}), bf16[8,4,64,192]{3,2,1,0:T(8,128)(2,1)S(1)}, u32[]{:S(2)}, u32[]{:S(2)}) async-start(bf16[8,4,64,192]{3,2,1,0:T(8,128)(2,1)} %stack.10), calls=%async_computation | async-start | bytes 2097152 | tf_op jit(solution)/shard_map/all_to_all | solution.py:63
  32.8 76.5 %reduce-scatter.10.cloned.1.call-start = ((), (), s32[]{:S(2)}) async-start(), calls=%async_computation.5 | async-start | bytes 1769472
  36.1 10.6 %copy-start.8 = (f32[1,4,20,128]{3,2,1,0:T(8,128)S(1)}, f32[1,4,20,128]{3,2,1,0:T(8,128)}, u32[]{:S(2)}) copy-start(f32[1,4,20,128]{3,2,1,0:T(8,128)} %broadcast_bitcast_fusion) | copy-start | bytes 122884
  46.8 1.0 copy-start.5
  50.5 8.4 %copy-start = (bf16[256,1536]{1,0:T(8,128)(2,1)}, bf16[256,1536]{1,0:T(8,128)(2,1)S(1)}, u32[]{:S(2)}) copy-start(bf16[256,1536]{1,0:T(8,128)(2,1)S(1)} %reshape_reshape.3) | copy-start | bytes 2359300
  59.0 1.2 copy-start.3
  72.5 123.8 %reduce-scatter.12.cloned.1.call-start = ((), (), s32[]{:S(2)}) async-start(), calls=%async_computation.6 | async-start | bytes 4177920
  114.9 1.1 copy-start.1
  114.9 1.6 copy-start.4
  115.0 222.5 %reduce-scatter.8.cloned.1.call-start = ((), (), s32[]{:S(2)}) async-start(), calls=%async_computation.4 | async-start | bytes 16711680 | tf_op jit(solution)/shard_map/reduce_scatter | solution.py:116
  337.5 68.2 %copy-start.6 = (f32[96,2560]{1,0:T(8,128)S(1)}, f32[96,2560]{1,0:T(8,128)}, u32[]{:S(2)}) copy-start(f32[96,2560]{1,0:T(8,128)} %reduce-scatter.8.cloned.1.call-done) | copy-start | bytes 2949124
Sparse Core Ops, SparseCore 0:
  72.6 36.6 reduce-scatter.9
  115.1 81.1 reduce-scatter.11
  200.7 136.7 reduce-scatter.7
